TPU v7x, 32 devices: a whole 2x2x4 slice. The times are simulated.
32 devices in a mesh: lon: 8 (over y, x, core), lat: 4 (over z).
Axes of the slice: x: 2, y: 2, z: 4, core: 2. Of those that a mesh axis runs over, the one named last changes fastest.
Arguments:
- background: bfloat16 [128, 512, 256], P('lat', 'lon'), may hold values from -6 to 6
- observations: bfloat16 [32768, 128], P(('lon', 'lat')), may hold values from -6 to 6
- w_station: bfloat16 [128, 256], replicated, may hold values from -0.5 to 0.5
- w_first: bfloat16 [3, 3, 256, 256], replicated, may hold values from -0.125 to 0.125
- w_second: bfloat16 [4, 4, 256, 256], replicated, may hold values from -0.09375 to 0.09375
- cotangent: bfloat16 [64, 256, 256], P('lat', 'lon'), may hold values from -6 to 6
- station_tile: int32 [32768, 1], P(('lon', 'lat')), may hold values from 0 to 31; in each aligned block of 1024 rows (0 to 1023, 1024 to 2047, ...) at most 64 rows name the same one
- station_cell: int32 [32768], P(('lon', 'lat')), may hold values from 0 to 2047
Outputs:
- encoded: bfloat16 [64, 256, 256], P('lat', 'lon')
- station_grad: bfloat16 [32768, 128], P(('lon', 'lat'))
- weight_grad: float32 [128, 256], replicated
Inputs may be any that keep to these rules, and one draw needn't show every extreme that they name: `station_tile`: tiles are numbered in the mesh's device order, longitude index times 4 plus latitude index. Among the 1024 observations that one device holds (aligned blocks), at most 64 name the same tile, and in every draw some device's observations name one tile exactly 64 times. `station_cell`: cell within the observation's tile, row-major over 32 x 64 cells.
All inputs are finite; a program needn't handle non-finite values.
Results may differ from a plain program's by a relative error of at most 0.0061.
Values may be sent and summed in bfloat16 or wider, within the bound.
No kernel may reach another device: no remote copies, remote signals or barrier semaphores. Data moves between devices by JAX's collectives and lax.ppermute only.
A program may use at most 64 MiB of HBM per device.

v0:
```python
import math

import jax
import jax.numpy as jnp
from jax import lax
from jax.sharding import PartitionSpec as P

def padded_2(cells, sides, width, closed):
    for axis, dim in sides:
        count = lax.axis_size(axis)
        ends = count if closed else count - 1
        head = lax.slice_in_dim(cells, 0, width, axis=dim)
        tail = lax.slice_in_dim(cells, cells.shape[dim] - width, cells.shape[dim], axis=dim)
        cells = jnp.concatenate(
            [
                lax.ppermute(tail, axis, [(i, (i + 1) % count) for i in range(ends)]),
                cells,
                lax.ppermute(head, axis, [((i + 1) % count, i) for i in range(ends)]),
            ],
            axis=dim,
        )
    return cells


def activate(values):
    return jax.nn.gelu(values, approximate=True)


def activate_back(values, upstream):
    return jax.vjp(activate, values)[1](upstream)[0]


def widen(grid_field, width):
    lon_sides = padded_2(grid_field, (("lon", 1),), width, True)
    return padded_2(lon_sides, (("lat", 0),), width, False)


def inside_rows(field):
    lat_index = lax.axis_index("lat")
    last = lax.axis_size("lat") - 1
    rows = jnp.arange(field.shape[0])[:, None, None]
    outside = ((rows == 0) & (lat_index == 0)) | ((rows == field.shape[0] - 1) & (lat_index == last))
    return jnp.where(outside, jnp.zeros_like(field), field)


def conv_valid(padded, kernel, stride, dilation, spec, rim=0):
    result = lax.conv_general_dilated(
        padded[None],
        kernel,
        (stride, stride),
        ((rim, rim), (rim, rim)),
        lhs_dilation=(dilation, dilation),
        dimension_numbers=("NHWC", spec, "NHWC"),
        preferred_element_type=jnp.float32,
    )
    return result[0]


def conv_three(padded, weight):
    return conv_valid(padded, weight, 1, 1, "HWIO")


def conv_stride(padded, weight):
    return conv_valid(padded, weight, 2, 1, "HWIO")


def conv_three_back(extended, weight):
    return conv_valid(extended, weight[::-1, ::-1], 1, 1, "HWOI")


def conv_stride_back(extended, weight):
    return conv_valid(extended, weight[::-1, ::-1], 1, 2, "HWOI", 1)


def send_out(payload, cell_ids, lon_count, lat_count, capacity):
    feature_width = payload.shape[1]
    got_load, got_cells = (
        lax.all_to_all(
            payload.reshape(lon_count * lat_count, capacity, feature_width),
            ("lon", "lat"),
            split_axis=0,
            concat_axis=0,
            tiled=True,
        ),
        lax.all_to_all(
            cell_ids.reshape(lon_count * lat_count, capacity),
            ("lon", "lat"),
            split_axis=0,
            concat_axis=0,
            tiled=True,
        ),
    )
    return (got_load.reshape(-1, feature_width), got_cells.reshape(-1))


def send_back(reply_rows, lon_count, lat_count, capacity):
    feature_width = reply_rows.shape[1]
    returned = lax.all_to_all(
        reply_rows.reshape(lon_count * lat_count, capacity, feature_width),
        ("lon", "lat"),
        split_axis=0,
        concat_axis=0,
        tiled=True,
    )
    return returned.reshape(-1, feature_width)


def sum_over_devices(term, count):
    rows, width = term.shape
    if rows % count != 0:
        return lax.psum(term, ("lon", "lat"))
    pieces = term.reshape(count, rows // count, width)
    gathered = lax.all_to_all(pieces, ("lon", "lat"), split_axis=0, concat_axis=0, tiled=True)
    own = jnp.sum(gathered, axis=0, keepdims=True)
    spread = jnp.broadcast_to(own, (count, rows // count, width))
    whole = lax.all_to_all(spread, ("lon", "lat"), split_axis=0, concat_axis=0, tiled=True)
    return whole.reshape(rows, width)


def on_device(
    background, observations, w_station, w_first, w_second, cotangent, station_tile, station_cell
):
    lon_count = lax.axis_size("lon")
    lat_count = lax.axis_size("lat")
    tile_count = lon_count * lat_count
    height, breadth, channels = background.shape
    tile_cells = height * breadth
    station_count = observations.shape[0]
    capacity = 2 * station_count // tile_count
    slot_total = tile_count * capacity
    target_tile = station_tile[:, 0]
    matches = (target_tile[:, None] == jnp.arange(tile_count, dtype=jnp.int32)[None, :]).astype(
        jnp.int32
    )
    earlier = jnp.cumsum(matches, axis=0) - matches
    flat_slot = target_tile * capacity + jnp.sum(earlier * matches, axis=1)
    send_cells = jnp.full((slot_total,), -1, jnp.int32).at[flat_slot].set(station_cell)
    station_pre = jnp.dot(observations, w_station, preferred_element_type=jnp.float32)
    payload = activate(station_pre).astype(jnp.bfloat16)
    send_rows = jnp.zeros((slot_total, payload.shape[1]), jnp.bfloat16).at[flat_slot].set(payload)
    got_load, got_cells = send_out(send_rows, send_cells, lon_count, lat_count, capacity)
    cell_match = (jnp.arange(tile_cells, dtype=jnp.int32)[:, None] == got_cells[None, :]).astype(
        jnp.bfloat16
    )
    assimilated = jnp.dot(cell_match, got_load, preferred_element_type=jnp.float32)
    state = background.reshape(tile_cells, channels).astype(jnp.float32) + assimilated
    state = state.astype(jnp.bfloat16).reshape(height, breadth, channels)
    state_rim = widen(state, 2)
    cotangent_rim = widen(cotangent, 1)
    first_pre = conv_three(state_rim, w_first)
    state_near = state_rim[1:-1, 1:-1].astype(jnp.float32)
    hidden = inside_rows((state_near + activate(first_pre)).astype(jnp.bfloat16))
    encoded = conv_stride(hidden, w_second).astype(jnp.bfloat16)
    hidden_grad = conv_stride_back(cotangent_rim, w_second)
    first_grad = inside_rows(activate_back(first_pre, hidden_grad).astype(jnp.bfloat16))
    state_grad = hidden_grad[1:-1, 1:-1] + conv_three_back(first_grad, w_first)
    state_grad = state_grad.astype(jnp.bfloat16).reshape(tile_cells, channels)
    arrived_grad = lax.dot_general(
        cell_match, state_grad, (((0,), (0,)), ((), ())), preferred_element_type=jnp.float32
    )
    returned = send_back(arrived_grad.astype(jnp.bfloat16), lon_count, lat_count, capacity)
    station_back = activate_back(station_pre, returned[flat_slot].astype(jnp.float32)).astype(
        jnp.bfloat16
    )
    station_grad = lax.dot_general(
        station_back, w_station, (((1,), (1,)), ((), ())), preferred_element_type=jnp.float32
    ).astype(jnp.bfloat16)
    weight_term = lax.dot_general(
        observations, station_back, (((0,), (0,)), ((), ())), preferred_element_type=jnp.float32
    )
    weight_grad = sum_over_devices(weight_term, tile_count)
    weight_grad = weight_grad * (1.0 / math.sqrt(station_count * tile_count))
    return (encoded, station_grad, weight_grad)


def solution(mesh):
    in_specs = (
        P("lat", "lon", None),
        P(("lon", "lat"), None),
        P(),
        P(),
        P(),
        P("lat", "lon", None),
        P(("lon", "lat"), None),
        P(("lon", "lat")),
    )
    out_specs = (P("lat", "lon", None), P(("lon", "lat"), None), P())
    return jax.shard_map(
        on_device, mesh=mesh, in_specs=in_specs, out_specs=out_specs, check_vma=False
    )
```

profile of v0, /device:TPU:0, one launch (start us, length us, event | category | flops | bytes accessed | tf_op | source)
XLA Modules:
  0.0 190.9 jit_solution(2247223706726771475)
XLA Ops:
  0.6 0.8 fusion.89
  1.5 9.0 %reduce-window.6 = s32[32,8,128]{2,1,0:T(8,128)S(1)} reduce-window(s32[32,8,128]{2,1,0:T(8,128)S(1)} %fusion.89, s32[]{:T(128)} %constant.16.clone.1), window={size=1x1x128 pad=0_0x0_0x127_0}, to_apply=%region_0.0 | reduce-window | flops 4161536 | bytes 262148 | tf_op jit(solution)/shard_map/reduce-window
  11.0 0.7 fusion.88
  11.7 0.7 compare_select_fusion
  12.4 4.5 %scatter_custom_fusion = s32[2048]{0:T(1024)S(1)} fusion(s32[1024]{0:T(1024)S(1)} %bitcast.128, s32[1024]{0:T(1024)} %param.15, s32[]{:T(128)} %constant.21.clone.1), kind=kCustom, calls=%fused_computation.125 | custom fusion | bytes 8704 | tf_op jit(solution)/shard_map/scatter | solution.py:137
  16.9 0.7 all_to_all.18
  17.6 7.3 %all-to-all-start = ((s32[32,1,64]{2,1,0:T(1,128)}), s32[32,1,64]{2,1,0:T(1,128)S(1)}, u32[]{:S(2)}, u32[]{:S(2)}) async-start(s32[32,1,64]{2,1,0:T(1,128)} %all_to_all.18), calls=%async_computation | async-start | bytes 32768 | tf_op jit(solution)/shard_map/all_to_all | solution.py:85
  24.9 1.3 fusion.108
  26.2 6.3 %scatter_custom_fusion.1 = bf16[2048,256]{1,0:T(8,128)(2,1)} fusion(s32[1024]{0:T(1024)S(1)} %bitcast.129, f32[1024,256]{1,0:T(8,128)S(1)} %fusion.108, f32[]{:T(128)} %constant.8.clone.1, f32[]{:T(128)} %constant.7.clone.1, f32[]{:T(128)} %constant.6.clone.1, f32[]{:T(128)} %constant.24.clone.1, bf16[]{:T(256)} %constant.20.clone.1), kind=kCustom, calls=%fused_computation.95 | custom fusion | flops 2359296 | bytes 2097170 | tf_op jit(solution)/shard_map/scatter | solution.py:140
  32.5 6.0 %all-to-all-start.1 = ((bf16[32,64,256]{2,1,0:T(8,128)(2,1)}), bf16[32,64,256]{2,1,0:T(8,128)(2,1)}, u32[]{:S(2)}, u32[]{:S(2)}) async-start(bf16[32,64,256]{2,1,0:T(8,128)(2,1)} %bitcast.116), calls=%async_computation.1 | async-start | bytes 2097152 | tf_op jit(solution)/shard_map/all_to_all | solution.py:78
  38.5 2.4 %collective-permute-start.5 = (bf16[16,1,256]{2,1,0:T(2,128)(2,1)S(1)}, bf16[16,1,256]{2,1,0:T(2,128)(2,1)S(1)}, u32[]{:S(2)}, u32[]{:S(2)}) collective-permute-start(bf16[16,1,256]{2,1,0:T(2,128)(2,1)S(1)} %get-tuple-element.21), channel_id=1, source_target_pairs={{4,0},{8,4},{12,8},{16,12},{20,16},{24,20},{28,24},{0,28},{5,1},{9... | collective-permute-start | bytes 24584 | tf_op jit(solution)/shard_map/ppermute | solution.py:18
  40.9 3.3 %collective-permute-done.5 = bf16[16,1,256]{2,1,0:T(2,128)(2,1)S(1)} collective-permute-done((bf16[16,1,256]{2,1,0:T(2,128)(2,1)S(1)}, bf16[16,1,256]{2,1,0:T(2,128)(2,1)S(1)}, u32[]{:S(2)}, u32[]{:S(2)}) %collective-permute-start.5) | collective-permute-done | bytes 8224 | tf_op jit(solution)/shard_map/ppermute | solution.py:18
  44.2 2.5 %collective-permute-done.4 = bf16[16,1,256]{2,1,0:T(2,128)(2,1)S(1)} collective-permute-done((bf16[16,1,256]{2,1,0:T(2,128)(2,1)S(1)}, bf16[16,1,256]{2,1,0:T(2,128)(2,1)S(1)}, u32[]{:S(2)}, u32[]{:S(2)}) %collective-permute-start.4) | collective-permute-done | bytes 8224 | tf_op jit(solution)/shard_map/ppermute | solution.py:16
  46.8 1.3 collective-permute-start.7
  48.1 4.5 %collective-permute-start.6 = (bf16[1,34,256]{2,1,0:T(8,128)(2,1)S(1)}, bf16[1,34,256]{2,1,0:T(8,128)(2,1)S(1)}, u32[]{:S(2)}, u32[]{:S(2)}) collective-permute-start(bf16[1,34,256]{2,1,0:T(8,128)(2,1)S(1)} %get-tuple-element.18), channel_id=1, source_target_pairs={{0,1},{1,2},{2,3},{4,5},{5,6},{6,7},{8,9},{9,10},{10,11},{12,13},{... | collective-permute-start | bytes 52232 | tf_op jit(solution)/shard_map/ppermute | solution.py:16
  52.6 0.5 and_or_fusion
  53.2 0.5 broadcast.258
  53.7 0.7 reduce.3
  54.4 1.9 %collective-permute-done.6 = bf16[1,34,256]{2,1,0:T(8,128)(2,1)S(1)} collective-permute-done((bf16[1,34,256]{2,1,0:T(8,128)(2,1)S(1)}, bf16[1,34,256]{2,1,0:T(8,128)(2,1)S(1)}, u32[]{:S(2)}, u32[]{:S(2)}) %collective-permute-start.6) | collective-permute-done | bytes 17440 | tf_op jit(solution)/shard_map/ppermute | solution.py:16
  56.8 6.7 %all-to-all-done.1 = bf16[32,64,256]{2,1,0:T(8,128)(2,1)} async-done(((bf16[32,64,256]{2,1,0:T(8,128)(2,1)}), bf16[32,64,256]{2,1,0:T(8,128)(2,1)}, u32[]{:S(2)}, u32[]{:S(2)}) %all-to-all-start.1) | async-done | bytes 1048608 | tf_op jit(solution)/shard_map/all_to_all | solution.py:78
  63.5 4.8 %fusion.21 = bf16[2048,256]{1,0:T(8,128)(2,1)S(1)} fusion(bf16[2048,256]{1,0:T(8,128)(2,1)} %bitcast.8, s32[2048]{0:T(1024)S(1)} %eq.79, bf16[2048,256]{1,0:T(8,128)(2,1)} %bitcast.131), kind=kOutput, calls=%fused_computation.37 | convolution fusion | flops 2153250816 | bytes 3153920 | tf_op jit(solution)/shard_map/dot_general | solution.py:145
  68.4 2.0 %collective-permute-start = (bf16[32,2,256]{2,0,1:T(8,128)(2,1)S(1)}, bf16[32,2,256]{2,0,1:T(8,128)(2,1)S(1)}, u32[]{:S(2)}, u32[]{:S(2)}) collective-permute-start(bf16[32,2,256]{2,0,1:T(8,128)(2,1)S(1)} %copy.92), channel_id=1, source_target_pairs={{0,4},{4,8},{8,12},{12,16},{16,20},{20,24},{24,28},{28,0},{1,5},{5... | collective-permute-start | bytes 98312 | tf_op jit(solution)/shard_map/ppermute | solution.py:16
  70.4 1.6 convolution_select_fusion
  72.0 1.6 copy.49
  73.7 1.2 collective-permute-start.1
  74.8 0.6 constant_dynamic-update-slice_fusion.1
  75.4 1.0 collective-permute-done.1
  76.6 1.3 collective-permute-start.3
  77.9 5.5 %collective-permute-start.2 = (bf16[2,68,256]{2,0,1:T(2,128)(2,1)S(1)}, bf16[2,68,256]{2,0,1:T(2,128)(2,1)S(1)}, u32[]{:S(2)}, u32[]{:S(2)}) collective-permute-start(bf16[2,68,256]{2,0,1:T(2,128)(2,1)S(1)} %get-tuple-element.14), channel_id=1, source_target_pairs={{0,1},{1,2},{2,3},{4,5},{5,6},{6,7},{8,9},{9,10},{10,11},{12,13},{... | collective-permute-start | bytes 208904 | tf_op jit(solution)/shard_map/ppermute | solution.py:16
  83.6 0.3 collective-permute-done.3
  83.9 1.4 collective-permute-done.2
  85.3 2.0 %pad_maximum_fusion = (bf16[36,68,256]{2,0,1:T(8,128)(2,1)}, bf16[36,1,68,256]{3,0,2,1:T(8,128)(2,1)S(1)}) fusion(bf16[2,68,256]{2,0,1:T(2,128)(2,1)S(1)} %collective-permute-done.3, bf16[32,68,256]{2,0,1:T(8,128)(2,1)S(1)} %constant_dynamic-update-slice_fusion, bf16[2,68,256]{2,0,1:T(2,128)(2,1)S(1)} %collective-permute-done.2), kind=kLoop, calls=%fused_computation.70 | loop fusion | flops 3760128 | bytes 3760128 | tf_op jit(solution)/shard_map/concatenate | solution.py:14
  87.8 0.8 copy-done.11
  88.6 3.8 %add_multiply_fusion = (f32[34,8,9,256]{3,1,2,0:T(8,128)S(1)}, f32[34,8,9,256]{3,1,2,0:T(8,128)S(1)}, f32[34,8,9,256]{3,1,2,0:T(8,128)S(1)}, f32[34,8,9,256]{3,1,2,0:T(8,128)S(1)}) fusion(bf16[3,3,256,256]{3,2,1,0:T(8,128)(2,1)S(1)} %copy-done.11, bf16[36,1,7,2,256]{4,2,3,0,1:T(8,128)(2,1)S(1)} %slice.65, bf16[36,1,8,9,256]{4,2,3,0,1:T(8,128)(2,1)S(1)} %copy.41, ...), kind=kOutput, calls=%fused_computation.44 | convolution fusion | flops 2899537920 | bytes 12791880 | tf_op jit(solution)/shard_map/conv_general_dilated | solution.py:47
  92.4 0.8 copy.42
  93.2 0.8 copy.55
  94.0 0.8 copy.53
  95.6 0.8 copy.50
  96.7 0.4 copy-done.9
  97.1 18.3 %select_bitcast_fusion = bf16[34,1,8,10,256]{4,2,3,0,1:T(8,128)(2,1)S(1)} fusion(pred[34]{0:T(512)(128)(4,1)S(1)} %copy-done.9, f32[34,8,10,256]{3,0,2,1:T(8,128)S(1)} %bitcast.105, f32[34,8,10,256]{3,0,2,1:T(8,128)S(1)} %bitcast.106, f32[34,8,10,256]{3,1,2,0:T(8,128)S(1)} %convolution_select_fusion, f32[34,8,10,256]{3,0,2,1:T(8,128)S(1)} %bitcast.107, ...), kind=kLoop, calls=%fused_computation.71 | loop fusion | flops 8355840 | bytes 15319154 | tf_op jit(solution)/shard_map/jit(_where)/select_n | solution.py:43
  115.5 3.6 %fusion.38 = f32[32,8,10,256]{3,1,2,0:T(8,128)S(1)} fusion(bf16[3,3,256,256]{3,2,1,0:T(8,128)(2,1)S(1)} %copy-done.11, bf16[34,1,7,2,256]{4,2,3,0,1:T(8,128)(2,1)S(1)} %slice.72, bf16[34,1,8,10,256]{4,2,3,0,1:T(8,128)(2,1)S(1)} %select_bitcast_fusion), kind=kOutput, calls=%fused_computation.56 | convolution fusion | flops 3024912384 | bytes 5437440 | tf_op jit(solution)/shard_map/conv_general_dilated | solution.py:47
  119.0 1.5 copy.57
  120.6 0.5 fusion.28
  121.1 0.6 copy.58
  121.7 5.5 %fusion.22 = bf16[2048,256]{1,0:T(8,128)(2,1)} fusion(bf16[2048,256]{1,0:T(8,128)(2,1)S(1)} %bitcast.122, s32[2048]{0:T(1024)S(1)} %eq.79), kind=kOutput, calls=%fused_computation.38 | convolution fusion | flops 2152202240 | bytes 2105344 | tf_op jit(solution)/shard_map/dot_general | solution.py:158
  127.2 5.0 %all-to-all-start.2 = ((bf16[32,64,256]{2,1,0:T(8,128)(2,1)}), bf16[32,64,256]{2,1,0:T(8,128)(2,1)S(1)}, u32[]{:S(2)}, u32[]{:S(2)}) async-start(bf16[32,64,256]{2,1,0:T(8,128)(2,1)} %bitcast.121), calls=%async_computation.2 | async-start | bytes 2097152 | tf_op jit(solution)/shard_map/all_to_all | solution.py:98
  132.3 3.5 %select_bitcast_fusion.1 = bf16[34,1,66,256]{3,0,2,1:T(8,128)(2,1)S(1)} fusion(f32[34,1,72,256]{3,0,2,1:T(8,128)} %bitcast.104, bf16[36,68,256]{2,0,1:T(8,128)(2,1)} %get-tuple-element.12, pred[34]{0:T(512)(128)(4,1)S(1)} %copy-done.9), kind=kLoop, calls=%fused_computation.72 | loop fusion | flops 6893568 | bytes 4595746 | tf_op jit(solution)/shard_map/broadcast_in_dim | solution.py:48
  135.9 0.5 copy.44
  136.4 1.1 copy-done.3
  137.5 0.9 slice.67
  138.3 19.0 %all-to-all-done.2 = bf16[32,64,256]{2,1,0:T(8,128)(2,1)S(1)} async-done(((bf16[32,64,256]{2,1,0:T(8,128)(2,1)}), bf16[32,64,256]{2,1,0:T(8,128)(2,1)S(1)}, u32[]{:S(2)}, u32[]{:S(2)}) %all-to-all-start.2) | async-done | bytes 1048608 | tf_op jit(solution)/shard_map/all_to_all | solution.py:98
  157.3 5.0 %gather_fusion = bf16[1024,256]{1,0:T(8,128)(2,1)} fusion(bf16[2048,256]{1,0:T(8,128)(2,1)S(1)} %bitcast.102, s32[1024]{0:T(1024)S(1)} %broadcast_clamp_fusion), kind=kCustom, calls=%fused_computation | custom fusion | bytes 1052672 | tf_op jit(solution)/shard_map/gather | solution.py:162
  162.2 2.1 %fusion.61 = bf16[1024,256]{1,0:T(8,128)(2,1)S(1)} fusion(bf16[1024,256]{1,0:T(8,128)(2,1)} %gather_fusion, f32[1024,256]{1,0:T(8,128)} %copy-done.2), kind=kLoop, calls=%fused_computation.81 | loop fusion | flops 5505024 | bytes 2097152 | tf_op jit(solution)/shard_map/convert_element_type | solution.py:162
  164.4 0.3 convolution_bitcast_fusion
  164.7 0.7 reshape.80
  165.4 4.4 %all-to-all-start.3 = ((f32[32,4,256]{2,1,0:T(4,128)}), f32[32,4,256]{2,1,0:T(4,128)S(1)}, u32[]{:S(2)}, u32[]{:S(2)}) async-start(f32[32,4,256]{2,1,0:T(4,128)} %reshape.80), calls=%async_computation.3 | async-start | bytes 262144 | tf_op jit(solution)/shard_map/all_to_all | solution.py:113
  169.9 3.0 %fusion.56 = bf16[16,8,5,256]{3,1,2,0:T(8,128)(2,1)S(1)} fusion(bf16[4,4,256,256]{3,2,1,0:T(8,128)(2,1)S(1)} %copy-done, bf16[34,1,7,3,256]{4,2,3,0,1:T(8,128)(2,1)} %slice.67, bf16[34,1,8,10,256]{4,2,3,0,1:T(8,128)(2,1)} %copy-done.3, pred[8,5]{0,1:T(8,128)(4,1)S(1)} %copy-done.13), kind=kOutput, calls=%fused_computation.76 | convolution fusion | flops 1347936256 | bytes 4183080 | tf_op jit(solution)/shard_map/conv_general_dilated | solution.py:47
  172.9 5.3 %all-to-all-done.3 = f32[32,4,256]{2,1,0:T(4,128)S(1)} async-done(((f32[32,4,256]{2,1,0:T(4,128)}), f32[32,4,256]{2,1,0:T(4,128)S(1)}, u32[]{:S(2)}, u32[]{:S(2)}) %all-to-all-start.3) | async-done | bytes 131104 | tf_op jit(solution)/shard_map/all_to_all | solution.py:113
  178.3 0.7 broadcast_in_dim.49
  179.0 2.6 %all-to-all-start.4 = ((f32[32,4,256]{2,1,0:T(4,128)}), f32[32,4,256]{2,1,0:T(4,128)S(1)}, u32[]{:S(2)}, u32[]{:S(2)}) async-start(f32[32,4,256]{2,1,0:T(4,128)} %broadcast_in_dim.49), calls=%async_computation.4 | async-start | bytes 262144 | tf_op jit(solution)/shard_map/all_to_all | solution.py:116
  181.6 0.8 copy.59
  182.4 1.0 convolution_convert_fusion
  183.4 6.6 %all-to-all-done.4 = f32[32,4,256]{2,1,0:T(4,128)S(1)} async-done(((f32[32,4,256]{2,1,0:T(4,128)}), f32[32,4,256]{2,1,0:T(4,128)S(1)}, u32[]{:S(2)}, u32[]{:S(2)}) %all-to-all-start.4) | async-done | bytes 131104 | tf_op jit(solution)/shard_map/all_to_all | solution.py:116
  190.0 0.7 mul.169
  (64 shorter events, 3.1 us)
Async XLA Ops:
  0.6 69.7 %copy-start = (bf16[4,4,256,256]{3,2,1,0:T(8,128)(2,1)S(1)}, bf16[4,4,256,256]{3,2,1,0:T(8,128)(2,1)}, u32[]{:S(2)}) copy-start(bf16[4,4,256,256]{3,2,1,0:T(8,128)(2,1)} %param.12) | copy-start | bytes 6291460
  12.4 20.1 %copy-start.7 = (s32[1024,1]{0,1:T(1,128)}, s32[1024,1]{0,1:T(1,128)S(1)}, u32[]{:S(2)}) copy-start(s32[1024,1]{0,1:T(1,128)S(1)} %compare_select_fusion) | copy-start | bytes 12292
  17.6 14.9 %all-to-all-start = ((s32[32,1,64]{2,1,0:T(1,128)}), s32[32,1,64]{2,1,0:T(1,128)S(1)}, u32[]{:S(2)}, u32[]{:S(2)}) async-start(s32[32,1,64]{2,1,0:T(1,128)} %all_to_all.18), calls=%async_computation | async-start | bytes 32768 | tf_op jit(solution)/shard_map/all_to_all | solution.py:85
  24.9 13.6 %copy-start.4 = (bf16[16,32,256]{2,1,0:T(8,128)(2,1)S(1)}, bf16[16,32,256]{2,1,0:T(8,128)(2,1)}, u32[]{:S(2)}) copy-start(bf16[16,32,256]{2,1,0:T(8,128)(2,1)} %param.13) | copy-start | bytes 786436
  26.2 30.4 %copy-start.2 = (f32[1024,256]{1,0:T(8,128)}, f32[1024,256]{1,0:T(8,128)S(1)}, u32[]{:S(2)}) copy-start(f32[1024,256]{1,0:T(8,128)S(1)} %fusion.108) | copy-start | bytes 3145732
  32.5 31.0 %all-to-all-start.1 = ((bf16[32,64,256]{2,1,0:T(8,128)(2,1)}), bf16[32,64,256]{2,1,0:T(8,128)(2,1)}, u32[]{:S(2)}, u32[]{:S(2)}) async-start(bf16[32,64,256]{2,1,0:T(8,128)(2,1)} %bitcast.116), calls=%async_computation.1 | async-start | bytes 2097152 | tf_op jit(solution)/shard_map/all_to_all | solution.py:78
  38.5 5.7 %collective-permute-start.5 = (bf16[16,1,256]{2,1,0:T(2,128)(2,1)S(1)}, bf16[16,1,256]{2,1,0:T(2,128)(2,1)S(1)}, u32[]{:S(2)}, u32[]{:S(2)}) collective-permute-start(bf16[16,1,256]{2,1,0:T(2,128)(2,1)S(1)} %get-tuple-element.21), channel_id=1, source_target_pairs={{4,0},{8,4},{12,8},{16,12},{20,16},{24,20},{28,24},{0,28},{5,1},{9... | collective-permute-start | bytes 24584 | tf_op jit(solution)/shard_map/ppermute | solution.py:18
  40.9 5.9 %collective-permute-start.4 = (bf16[16,1,256]{2,1,0:T(2,128)(2,1)S(1)}, bf16[16,1,256]{2,1,0:T(2,128)(2,1)S(1)}, u32[]{:S(2)}, u32[]{:S(2)}) collective-permute-start(bf16[16,1,256]{2,1,0:T(2,128)(2,1)S(1)} %get-tuple-element.20), channel_id=1, source_target_pairs={{0,4},{4,8},{8,12},{12,16},{16,20},{20,24},{24,28},{28,0},{1,5},{5... | collective-permute-start | bytes 24584 | tf_op jit(solution)/shard_map/ppermute | solution.py:16
  46.8 7.7 %collective-permute-start.7 = (bf16[1,34,256]{2,1,0:T(8,128)(2,1)S(1)}, bf16[1,34,256]{2,1,0:T(8,128)(2,1)S(1)}, u32[]{:S(2)}, u32[]{:S(2)}) collective-permute-start(bf16[1,34,256]{2,1,0:T(8,128)(2,1)S(1)} %get-tuple-element.19), channel_id=1, source_target_pairs={{1,0},{2,1},{3,2},{5,4},{6,5},{7,6},{9,8},{10,9},{11,10},{13,12},{... | collective-permute-start | bytes 52232 | tf_op jit(solution)/shard_map/ppermute | solution.py:18
  48.1 8.3 %collective-permute-start.6 = (bf16[1,34,256]{2,1,0:T(8,128)(2,1)S(1)}, bf16[1,34,256]{2,1,0:T(8,128)(2,1)S(1)}, u32[]{:S(2)}, u32[]{:S(2)}) collective-permute-start(bf16[1,34,256]{2,1,0:T(8,128)(2,1)S(1)} %get-tuple-element.18), channel_id=1, source_target_pairs={{0,1},{1,2},{2,3},{4,5},{5,6},{6,7},{8,9},{9,10},{10,11},{12,13},{... | collective-permute-start | bytes 52232 | tf_op jit(solution)/shard_map/ppermute | solution.py:16
  63.5 6.9 %copy-start.10 = (pred[8,10]{0,1:T(8,128)(4,1)S(1)}, pred[8,10]{0,1:T(8,128)(4,1)}, u32[]{:S(2)}) copy-start(pred[8,10]{0,1:T(8,128)(4,1)} %constant.68) | copy-start | bytes 244
  68.4 6.5 %collective-permute-start = (bf16[32,2,256]{2,0,1:T(8,128)(2,1)S(1)}, bf16[32,2,256]{2,0,1:T(8,128)(2,1)S(1)}, u32[]{:S(2)}, u32[]{:S(2)}) collective-permute-start(bf16[32,2,256]{2,0,1:T(8,128)(2,1)S(1)} %copy.92), channel_id=1, source_target_pairs={{0,4},{4,8},{8,12},{12,16},{16,20},{20,24},{24,28},{28,0},{1,5},{5... | collective-permute-start | bytes 98312 | tf_op jit(solution)/shard_map/ppermute | solution.py:16
  73.7 2.8 %collective-permute-start.1 = (bf16[32,2,256]{2,0,1:T(8,128)(2,1)S(1)}, bf16[32,2,256]{2,0,1:T(8,128)(2,1)S(1)}, u32[]{:S(2)}, u32[]{:S(2)}) collective-permute-start(bf16[32,2,256]{2,0,1:T(8,128)(2,1)S(1)} %copy.93), channel_id=1, source_target_pairs={{4,0},{8,4},{12,8},{16,12},{20,16},{24,20},{28,24},{0,28},{5,1},{9... | collective-permute-start | bytes 98312 | tf_op jit(solution)/shard_map/ppermute | solution.py:18
  76.6 7.3 %collective-permute-start.3 = (bf16[2,68,256]{2,0,1:T(2,128)(2,1)S(1)}, bf16[2,68,256]{2,0,1:T(2,128)(2,1)S(1)}, u32[]{:S(2)}, u32[]{:S(2)}) collective-permute-start(bf16[2,68,256]{2,0,1:T(2,128)(2,1)S(1)} %get-tuple-element.15), channel_id=1, source_target_pairs={{1,0},{2,1},{3,2},{5,4},{6,5},{7,6},{9,8},{10,9},{11,10},{13,12},{... | collective-permute-start | bytes 208904 | tf_op jit(solution)/shard_map/ppermute | solution.py:18
  77.9 7.4 %collective-permute-start.2 = (bf16[2,68,256]{2,0,1:T(2,128)(2,1)S(1)}, bf16[2,68,256]{2,0,1:T(2,128)(2,1)S(1)}, u32[]{:S(2)}, u32[]{:S(2)}) collective-permute-start(bf16[2,68,256]{2,0,1:T(2,128)(2,1)S(1)} %get-tuple-element.14), channel_id=1, source_target_pairs={{0,1},{1,2},{2,3},{4,5},{5,6},{6,7},{8,9},{9,10},{10,11},{12,13},{... | collective-permute-start | bytes 208904 | tf_op jit(solution)/shard_map/ppermute | solution.py:16
  87.3 1.3 copy-start.11
  87.3 1.3 copy-start.12
  93.2 2.2 %copy-start.1 = (f32[34,8,9,256]{3,0,2,1:T(8,128)}, f32[34,8,9,256]{3,0,2,1:T(8,128)S(1)}, u32[]{:S(2)}) copy-start(f32[34,8,9,256]{3,0,2,1:T(8,128)S(1)} %copy.42) | copy-start | bytes 7520260
  96.4 0.7 copy-start.9
  121.7 10.6 %copy-start.8 = (s32[1024,1]{0,1:T(1,128)S(1)}, s32[1024,1]{0,1:T(1,128)}, u32[]{:S(2)}) copy-start(s32[1024,1]{0,1:T(1,128)} %copy-done.7) | copy-start | bytes 12292
  127.2 30.1 %all-to-all-start.2 = ((bf16[32,64,256]{2,1,0:T(8,128)(2,1)}), bf16[32,64,256]{2,1,0:T(8,128)(2,1)S(1)}, u32[]{:S(2)}, u32[]{:S(2)}) async-start(bf16[32,64,256]{2,1,0:T(8,128)(2,1)} %bitcast.121), calls=%async_computation.2 | async-start | bytes 2097152 | tf_op jit(solution)/shard_map/all_to_all | solution.py:98
  136.4 1.1 copy-start.3
  157.3 7.1 %copy-start.5 = (bf16[1024,128]{1,0:T(8,128)(2,1)S(1)}, bf16[1024,128]{1,0:T(8,128)(2,1)}, u32[]{:S(2)}) copy-start(bf16[1024,128]{1,0:T(8,128)(2,1)} %param.9) | copy-start | bytes 786436
  162.2 7.6 %copy-start.13 = (pred[8,5]{0,1:T(8,128)(4,1)S(1)}, pred[8,5]{0,1:T(8,128)(4,1)}, u32[]{:S(2)}) copy-start(pred[8,5]{0,1:T(8,128)(4,1)} %constant.66) | copy-start | bytes 124
  165.4 12.9 %all-to-all-start.3 = ((f32[32,4,256]{2,1,0:T(4,128)}), f32[32,4,256]{2,1,0:T(4,128)S(1)}, u32[]{:S(2)}, u32[]{:S(2)}) async-start(f32[32,4,256]{2,1,0:T(4,128)} %reshape.80), calls=%async_computation.3 | async-start | bytes 262144 | tf_op jit(solution)/shard_map/all_to_all | solution.py:113
  169.8 12.5 %copy-start.6 = (bf16[128,256]{1,0:T(8,128)(2,1)S(1)}, bf16[128,256]{1,0:T(8,128)(2,1)}, u32[]{:S(2)}) copy-start(bf16[128,256]{1,0:T(8,128)(2,1)} %param.10) | copy-start | bytes 196612
  179.0 11.0 %all-to-all-start.4 = ((f32[32,4,256]{2,1,0:T(4,128)}), f32[32,4,256]{2,1,0:T(4,128)S(1)}, u32[]{:S(2)}, u32[]{:S(2)}) async-start(f32[32,4,256]{2,1,0:T(4,128)} %broadcast_in_dim.49), calls=%async_computation.4 | async-start | bytes 262144 | tf_op jit(solution)/shard_map/all_to_all | solution.py:116
where the time goes:
time: 193 us; the launch traced here: 191 us
  waiting for transfers between devices  48.1 us (25%)
  other arithmetic  45.6 us (24%)
  starting transfers between devices  43.5 us (23%)
  local copies, waits for them, and re-layouts  27.4 us (14%)
  matrix products  24.9 us (13%)
    all_to_all x1, waiting for transfers between devices, send_back(): lax.all_to_all(reply_rows.reshape(lon_count * lat_count, capacity, featur...  19 us
    select_n x1, other arithmetic, inside_rows(): return jnp.where(outside, jnp.zeros_like(field), field)  18.3 us
    ppermute x4, starting transfers between devices, padded_2(): lax.ppermute(tail, axis, [(i, (i + 1) % count) for i in range(ends)])  12 us
    conv_general_dilated x4, matrix products, conv_valid(): lax.conv_general_dilated(padded[None], kernel, (stride, stride), ((rim, r...  12 us
    another operation x3, other arithmetic  9.15 us
    all_to_all x1, starting transfers between devices, send_out(): lax.all_to_all(cell_ids.reshape(lon_count * lat_count, capacity), ('lon',...  7.3 us
    all_to_all x1, waiting for transfers between devices, send_out(): lax.all_to_all(payload.reshape(lon_count * lat_count, capacity, feature_w...  6.67 us
    all_to_all x1, waiting for transfers between devices, sum_over_devices(): lax.all_to_all(spread, ('lon', 'lat'), split_axis=0, concat_axis=0, tiled...  6.59 us
  transfers between devices with their start and end apart: 13, of which 10 were waited for; matrix products, arithmetic and copies ran while one was open for 12% of the time, Pallas kernels for 0%

commit v1 on v0

--- a/solution.py
+++ b/solution.py
@@ -152,7 +152,8 @@
     hidden = inside_rows((state_near + activate(first_pre)).astype(jnp.bfloat16))
     encoded = conv_stride(hidden, w_second).astype(jnp.bfloat16)
     hidden_grad = conv_stride_back(cotangent_rim, w_second)
-    first_grad = inside_rows(activate_back(first_pre, hidden_grad).astype(jnp.bfloat16))
+    first_pre_again = lax.optimization_barrier(first_pre)
+    first_grad = inside_rows(activate_back(first_pre_again, hidden_grad).astype(jnp.bfloat16))
     state_grad = hidden_grad[1:-1, 1:-1] + conv_three_back(first_grad, w_first)
     state_grad = state_grad.astype(jnp.bfloat16).reshape(tile_cells, channels)
     arrived_grad = lax.dot_general(

time: 193 us -> 172 us (0.89)
  other arithmetic: 45.6 us -> 26.9 us
  waiting for transfers between devices: 48.1 us -> 53.9 us
  starting transfers between devices: 43.5 us -> 39.6 us
  local copies, waits for them, and re-layouts: 27.4 us -> 25.4 us
    select_n x1 -> x0, other arithmetic: 18.3 us -> none  [inside_rows(): return jnp.where(outside, jnp.zeros_like(field), field)]
    ppermute x4, waiting for transfers between devices: 5.91 us -> 9.24 us  [padded_2(): lax.ppermute(tail, axis, [(i, (i + 1) % count) for i in range(ends)])]
    mul x6 -> x0, local copies, waits for them, and re-layouts: 3.17 us -> none  [activate(): return jax.nn.gelu(values, approximate=True)]
    all_to_all x1, starting transfers between devices: 5.04 us -> 2.9 us  [send_back(): lax.all_to_all(reply_rows.reshape(lon_count * lat_count, capacity, featur...]
    concatenate x1 -> x0, other arithmetic: 1.99 us -> none  [padded_2(): jnp.concatenate([lax.ppermute(tail, axis, [(i, (i + 1) % count) for i in...]
    broadcast_in_dim x2 -> x3, other arithmetic: 3.67 us -> 5.24 us  [conv_valid(): padded[None]]
    conv_general_dilated x10 -> x11, local copies, waits for them, and re-layouts: 5.99 us -> 5.34 us  [conv_valid(): lax.conv_general_dilated(padded[None], kernel, (stride, stride), ((rim, r...]
  transfers between devices with their start and end apart: 13 -> 13, of which waited for: 10 -> 9; matrix products, arithmetic and copies ran while one was open for 12% -> 13% of each run, Pallas kernels for 0% -> 0%
where the time goes in v1:
time: 172 us; the launch traced here: 171 us
  waiting for transfers between devices  53.9 us (31%)
  starting transfers between devices  39.6 us (23%)
  other arithmetic  26.9 us (16%)
  local copies, waits for them, and re-layouts  25.4 us (15%)
  matrix products  24.2 us (14%)
    all_to_all x1, waiting for transfers between devices, send_back(): lax.all_to_all(reply_rows.reshape(lon_count * lat_count, capacity, featur...  20.9 us
    conv_general_dilated x4, matrix products, conv_valid(): lax.conv_general_dilated(padded[None], kernel, (stride, stride), ((rim, r...  11.3 us
    ppermute x4, starting transfers between devices, padded_2(): lax.ppermute(tail, axis, [(i, (i + 1) % count) for i in range(ends)])  10.3 us
    ppermute x4, waiting for transfers between devices, padded_2(): lax.ppermute(tail, axis, [(i, (i + 1) % count) for i in range(ends)])  9.24 us
    another operation x3, other arithmetic  9.15 us
    all_to_all x1, starting transfers between devices, send_out(): lax.all_to_all(cell_ids.reshape(lon_count * lat_count, capacity), ('lon',...  7.3 us
    all_to_all x1, waiting for transfers between devices, send_out(): lax.all_to_all(payload.reshape(lon_count * lat_count, capacity, feature_w...  6.66 us
    all_to_all x1, waiting for transfers between devices, sum_over_devices(): lax.all_to_all(spread, ('lon', 'lat'), split_axis=0, concat_axis=0, tiled...  6.59 us
  transfers between devices with their start and end apart: 13, of which 9 were waited for; matrix products, arithmetic and copies ran while one was open for 13% of the time, Pallas kernels for 0%

profile of v1, /device:TPU:0, one launch (start us, length us, event | category | flops | bytes accessed | tf_op | source)
XLA Modules:
  0.0 171.2 jit_solution(18353932845086101224)
XLA Ops:
  0.6 0.8 fusion.87
  1.5 9.0 %reduce-window.6 = s32[32,8,128]{2,1,0:T(8,128)S(1)} reduce-window(s32[32,8,128]{2,1,0:T(8,128)S(1)} %fusion.87, s32[]{:T(128)} %constant.16.clone.1), window={size=1x1x128 pad=0_0x0_0x127_0}, to_apply=%region_0.0 | reduce-window | flops 4161536 | bytes 262148 | tf_op jit(solution)/shard_map/reduce-window
  11.0 0.7 fusion.86
  11.7 0.7 compare_select_fusion
  12.4 4.5 %scatter_custom_fusion = s32[2048]{0:T(1024)S(1)} fusion(s32[1024]{0:T(1024)S(1)} %bitcast.115, s32[1024]{0:T(1024)} %param.15, s32[]{:T(128)} %constant.21.clone.1), kind=kCustom, calls=%fused_computation.118 | custom fusion | bytes 8704 | tf_op jit(solution)/shard_map/scatter | solution.py:137
  16.9 0.7 all_to_all.18
  17.6 7.3 %all-to-all-start = ((s32[32,1,64]{2,1,0:T(1,128)}), s32[32,1,64]{2,1,0:T(1,128)S(1)}, u32[]{:S(2)}, u32[]{:S(2)}) async-start(s32[32,1,64]{2,1,0:T(1,128)} %all_to_all.18), calls=%async_computation | async-start | bytes 32768 | tf_op jit(solution)/shard_map/all_to_all | solution.py:85
  24.9 1.3 fusion.106
  26.2 6.3 %scatter_custom_fusion.1 = bf16[2048,256]{1,0:T(8,128)(2,1)} fusion(s32[1024]{0:T(1024)S(1)} %bitcast.116, f32[1024,256]{1,0:T(8,128)S(1)} %fusion.106, f32[]{:T(128)} %constant.8.clone.1, f32[]{:T(128)} %constant.7.clone.1, f32[]{:T(128)} %constant.6.clone.1, f32[]{:T(128)} %constant.24.clone.1, bf16[]{:T(256)} %constant.20.clone.1), kind=kCustom, calls=%fused_computation.88 | custom fusion | flops 2359296 | bytes 2097170 | tf_op jit(solution)/shard_map/scatter | solution.py:140
  32.5 6.0 %all-to-all-start.1 = ((bf16[32,64,256]{2,1,0:T(8,128)(2,1)}), bf16[32,64,256]{2,1,0:T(8,128)(2,1)}, u32[]{:S(2)}, u32[]{:S(2)}) async-start(bf16[32,64,256]{2,1,0:T(8,128)(2,1)} %bitcast.103), calls=%async_computation.1 | async-start | bytes 2097152 | tf_op jit(solution)/shard_map/all_to_all | solution.py:78
  38.5 0.2 collective-permute-start.4
  38.7 2.5 %collective-permute-start.5 = (bf16[16,1,256]{2,1,0:T(2,128)(2,1)S(1)}, bf16[16,1,256]{2,1,0:T(2,128)(2,1)S(1)}, u32[]{:S(2)}, u32[]{:S(2)}) collective-permute-start(bf16[16,1,256]{2,1,0:T(2,128)(2,1)S(1)} %get-tuple-element.18), channel_id=1, source_target_pairs={{4,0},{8,4},{12,8},{16,12},{20,16},{24,20},{28,24},{0,28},{5,1},{9... | collective-permute-start | bytes 24584 | tf_op jit(solution)/shard_map/ppermute | solution.py:18
  41.2 5.6 %collective-permute-done.4 = bf16[16,1,256]{2,1,0:T(2,128)(2,1)S(1)} collective-permute-done((bf16[16,1,256]{2,1,0:T(2,128)(2,1)S(1)}, bf16[16,1,256]{2,1,0:T(2,128)(2,1)S(1)}, u32[]{:S(2)}, u32[]{:S(2)}) %collective-permute-start.4) | collective-permute-done | bytes 8224 | tf_op jit(solution)/shard_map/ppermute | solution.py:16
  46.8 3.3 %collective-permute-start.6 = (bf16[1,34,256]{2,1,0:T(8,128)(2,1)S(1)}, bf16[1,34,256]{2,1,0:T(8,128)(2,1)S(1)}, u32[]{:S(2)}, u32[]{:S(2)}) collective-permute-start(bf16[1,34,256]{2,1,0:T(8,128)(2,1)S(1)} %get-tuple-element.15), channel_id=1, source_target_pairs={{0,1},{1,2},{2,3},{4,5},{5,6},{6,7},{8,9},{9,10},{10,11},{12,13},{... | collective-permute-start | bytes 52232 | tf_op jit(solution)/shard_map/ppermute | solution.py:16
  50.1 1.3 collective-permute-start.7
  51.4 0.5 and_or_fusion
  51.9 0.5 broadcast.217
  52.4 0.7 reduce.3
  53.2 3.2 %collective-permute-done.6 = bf16[1,34,256]{2,1,0:T(8,128)(2,1)S(1)} collective-permute-done((bf16[1,34,256]{2,1,0:T(8,128)(2,1)S(1)}, bf16[1,34,256]{2,1,0:T(8,128)(2,1)S(1)}, u32[]{:S(2)}, u32[]{:S(2)}) %collective-permute-start.6) | collective-permute-done | bytes 17440 | tf_op jit(solution)/shard_map/ppermute | solution.py:16
  56.8 6.7 %all-to-all-done.1 = bf16[32,64,256]{2,1,0:T(8,128)(2,1)} async-done(((bf16[32,64,256]{2,1,0:T(8,128)(2,1)}), bf16[32,64,256]{2,1,0:T(8,128)(2,1)}, u32[]{:S(2)}, u32[]{:S(2)}) %all-to-all-start.1) | async-done | bytes 1048608 | tf_op jit(solution)/shard_map/all_to_all | solution.py:78
  63.5 4.8 %fusion.24 = bf16[2048,256]{1,0:T(8,128)(2,1)S(1)} fusion(bf16[2048,256]{1,0:T(8,128)(2,1)} %bitcast.8, s32[2048]{0:T(1024)S(1)} %eq.79, bf16[2048,256]{1,0:T(8,128)(2,1)} %bitcast.118), kind=kOutput, calls=%fused_computation.36 | convolution fusion | flops 2153250816 | bytes 3153920 | tf_op jit(solution)/shard_map/dot_general | solution.py:145
  68.4 1.9 %collective-permute-start = (bf16[32,2,256]{2,0,1:T(8,128)(2,1)S(1)}, bf16[32,2,256]{2,0,1:T(8,128)(2,1)S(1)}, u32[]{:S(2)}, u32[]{:S(2)}) collective-permute-start(bf16[32,2,256]{2,0,1:T(8,128)(2,1)S(1)} %copy.54), channel_id=1, source_target_pairs={{0,4},{4,8},{8,12},{12,16},{16,20},{20,24},{24,28},{28,0},{1,5},{5... | collective-permute-start | bytes 98312 | tf_op jit(solution)/shard_map/ppermute | solution.py:16
  70.3 1.7 convolution_select_fusion
  72.0 1.6 copy.44
  73.6 1.1 collective-permute-start.1
  74.8 0.6 constant_dynamic-update-slice_fusion.1
  75.4 1.0 collective-permute-done.1
  76.5 4.9 %collective-permute-start.2 = (bf16[2,68,256]{2,0,1:T(2,128)(2,1)S(1)}, bf16[2,68,256]{2,0,1:T(2,128)(2,1)S(1)}, u32[]{:S(2)}, u32[]{:S(2)}) collective-permute-start(bf16[2,68,256]{2,0,1:T(2,128)(2,1)S(1)} %get-tuple-element.11), channel_id=1, source_target_pairs={{0,1},{1,2},{2,3},{4,5},{5,6},{6,7},{8,9},{9,10},{10,11},{12,13},{... | collective-permute-start | bytes 208904 | tf_op jit(solution)/shard_map/ppermute | solution.py:16
  81.4 1.3 collective-permute-start.3
  82.8 0.4 collective-permute-done.2
  83.3 4.3 %collective-permute-done.3 = bf16[2,68,256]{2,0,1:T(2,128)(2,1)S(1)} collective-permute-done((bf16[2,68,256]{2,0,1:T(2,128)(2,1)S(1)}, bf16[2,68,256]{2,0,1:T(2,128)(2,1)S(1)}, u32[]{:S(2)}, u32[]{:S(2)}) %collective-permute-start.3) | collective-permute-done | bytes 69664 | tf_op jit(solution)/shard_map/ppermute | solution.py:18
  87.6 0.9 fusion.102
  88.7 0.3 copy.36
  89.0 0.8 copy-done.9
  89.8 3.5 %fusion.42 = f32[34,8,9,256]{3,1,2,0:T(8,128)S(1)} fusion(bf16[3,3,256,256]{3,2,1,0:T(8,128)(2,1)S(1)} %copy-done.9, bf16[36,1,7,2,256]{4,2,3,0,1:T(8,128)(2,1)S(1)} %slice.65, bf16[36,1,8,9,256]{4,2,3,0,1:T(8,128)(2,1)S(1)} %copy.36, pred[8,9]{0,1:T(8,128)(4,1)S(1)} %copy-done.11), kind=kOutput, calls=%fused_computation.54 | convolution fusion | flops 2893271040 | bytes 5271624 | tf_op jit(solution)/shard_map/conv_general_dilated | solution.py:47
  93.3 0.8 copy.37
  94.3 0.5 copy-done.8
  94.8 4.1 %select_bitcast_fusion = (bf16[34,1,66,256]{3,0,2,1:T(8,128)(2,1)S(1)}, bf16[34,1,66,256]{3,0,2,1:T(8,128)(2,1)}) fusion(pred[34]{0:T(512)(128)(4,1)S(1)} %copy-done.8, f32[34,66,256]{2,0,1:T(8,128)S(1)} %slice_bitcast_fusion.1, f32[34,1,80,256]{3,0,2,1:T(8,128)S(1)} %bitcast.98, f32[34,1,72,256]{3,0,2,1:T(8,128)S(1)} %bitcast.96, ...), kind=kLoop, calls=%fused_computation.64 | loop fusion | flops 18957312 | bytes 10340386 | tf_op jit(solution)/shard_map/broadcast_in_dim | solution.py:48
  99.0 0.3 copy.46
  99.3 0.2 copy-done.10
  99.6 3.2 %convolution_select_fusion.1 = f32[32,8,9,256]{3,1,2,0:T(8,128)S(1)} fusion(bf16[3,3,256,256]{3,2,1,0:T(8,128)(2,1)S(1)} %copy-done.9, bf16[34,1,7,2,256]{4,2,3,0,1:T(8,128)(2,1)S(1)} %slice.72, bf16[34,1,8,9,256]{4,2,3,0,1:T(8,128)(2,1)S(1)} %copy.46, pred[8,9]{0,1:T(8,128)(4,1)S(1)} %copy-done.10), kind=kOutput, calls=%fused_computation.55 | convolution fusion | flops 2723094528 | bytes 5036104 | tf_op jit(solution)/shard_map/conv_general_dilated | solution.py:47
  102.8 0.8 copy.47
  103.5 0.5 fusion.27
  104.1 0.6 copy.48
  104.7 5.5 %fusion.25 = bf16[2048,256]{1,0:T(8,128)(2,1)} fusion(bf16[2048,256]{1,0:T(8,128)(2,1)S(1)} %bitcast.109, s32[2048]{0:T(1024)S(1)} %eq.79), kind=kOutput, calls=%fused_computation.37 | convolution fusion | flops 2152202240 | bytes 2105344 | tf_op jit(solution)/shard_map/dot_general | solution.py:159
  110.2 2.9 %all-to-all-start.2 = ((bf16[32,64,256]{2,1,0:T(8,128)(2,1)}), bf16[32,64,256]{2,1,0:T(8,128)(2,1)S(1)}, u32[]{:S(2)}, u32[]{:S(2)}) async-start(bf16[32,64,256]{2,1,0:T(8,128)(2,1)} %bitcast.108), calls=%async_computation.2 | async-start | bytes 2097152 | tf_op jit(solution)/shard_map/all_to_all | solution.py:98
  113.1 1.5 pad.2
  114.6 0.5 copy.39
  115.1 1.1 copy-done.2
  116.2 0.9 slice.67
  117.0 20.9 %all-to-all-done.2 = bf16[32,64,256]{2,1,0:T(8,128)(2,1)S(1)} async-done(((bf16[32,64,256]{2,1,0:T(8,128)(2,1)}), bf16[32,64,256]{2,1,0:T(8,128)(2,1)S(1)}, u32[]{:S(2)}, u32[]{:S(2)}) %all-to-all-start.2) | async-done | bytes 1048608 | tf_op jit(solution)/shard_map/all_to_all | solution.py:98
  137.9 5.0 %gather_fusion = bf16[1024,256]{1,0:T(8,128)(2,1)} fusion(bf16[2048,256]{1,0:T(8,128)(2,1)S(1)} %bitcast.94, s32[1024]{0:T(1024)S(1)} %broadcast_clamp_fusion), kind=kCustom, calls=%fused_computation | custom fusion | bytes 1052672 | tf_op jit(solution)/shard_map/gather | solution.py:163
  142.8 2.1 %fusion.59 = bf16[1024,256]{1,0:T(8,128)(2,1)S(1)} fusion(bf16[1024,256]{1,0:T(8,128)(2,1)} %gather_fusion, f32[1024,256]{1,0:T(8,128)} %copy-done.1), kind=kLoop, calls=%fused_computation.74 | loop fusion | flops 5505024 | bytes 2097152 | tf_op jit(solution)/shard_map/convert_element_type | solution.py:163
  145.0 0.3 convolution_bitcast_fusion
  145.3 0.7 reshape.80
  146.0 4.4 %all-to-all-start.3 = ((f32[32,4,256]{2,1,0:T(4,128)}), f32[32,4,256]{2,1,0:T(4,128)S(1)}, u32[]{:S(2)}, u32[]{:S(2)}) async-start(f32[32,4,256]{2,1,0:T(4,128)} %reshape.80), calls=%async_computation.3 | async-start | bytes 262144 | tf_op jit(solution)/shard_map/all_to_all | solution.py:113
  150.4 3.0 %fusion.54 = bf16[16,8,5,256]{3,1,2,0:T(8,128)(2,1)S(1)} fusion(bf16[4,4,256,256]{3,2,1,0:T(8,128)(2,1)S(1)} %copy-done, bf16[34,1,7,3,256]{4,2,3,0,1:T(8,128)(2,1)} %slice.67, bf16[34,1,8,10,256]{4,2,3,0,1:T(8,128)(2,1)} %copy-done.2, pred[8,5]{0,1:T(8,128)(4,1)S(1)} %copy-done.13), kind=kOutput, calls=%fused_computation.69 | convolution fusion | flops 1347936256 | bytes 4183080 | tf_op jit(solution)/shard_map/conv_general_dilated | solution.py:47
  153.5 5.3 %all-to-all-done.3 = f32[32,4,256]{2,1,0:T(4,128)S(1)} async-done(((f32[32,4,256]{2,1,0:T(4,128)}), f32[32,4,256]{2,1,0:T(4,128)S(1)}, u32[]{:S(2)}, u32[]{:S(2)}) %all-to-all-start.3) | async-done | bytes 131104 | tf_op jit(solution)/shard_map/all_to_all | solution.py:113
  158.8 0.7 broadcast_in_dim.49
  159.5 2.6 %all-to-all-start.4 = ((f32[32,4,256]{2,1,0:T(4,128)}), f32[32,4,256]{2,1,0:T(4,128)S(1)}, u32[]{:S(2)}, u32[]{:S(2)}) async-start(f32[32,4,256]{2,1,0:T(4,128)} %broadcast_in_dim.49), calls=%async_computation.4 | async-start | bytes 262144 | tf_op jit(solution)/shard_map/all_to_all | solution.py:116
  162.1 0.8 copy.49
  162.9 1.0 convolution_convert_fusion
  163.9 6.6 %all-to-all-done.4 = f32[32,4,256]{2,1,0:T(4,128)S(1)} async-done(((f32[32,4,256]{2,1,0:T(4,128)}), f32[32,4,256]{2,1,0:T(4,128)S(1)}, u32[]{:S(2)}, u32[]{:S(2)}) %all-to-all-start.4) | async-done | bytes 131104 | tf_op jit(solution)/shard_map/all_to_all | solution.py:116
  170.5 0.7 mul.157
  (59 shorter events, 2.1 us)
Async XLA Ops:
  0.6 69.7 %copy-start = (bf16[4,4,256,256]{3,2,1,0:T(8,128)(2,1)S(1)}, bf16[4,4,256,256]{3,2,1,0:T(8,128)(2,1)}, u32[]{:S(2)}) copy-start(bf16[4,4,256,256]{3,2,1,0:T(8,128)(2,1)} %param.12) | copy-start | bytes 6291460
  12.4 20.1 %copy-start.6 = (s32[1024,1]{0,1:T(1,128)}, s32[1024,1]{0,1:T(1,128)S(1)}, u32[]{:S(2)}) copy-start(s32[1024,1]{0,1:T(1,128)S(1)} %compare_select_fusion) | copy-start | bytes 12292
  17.6 14.9 %all-to-all-start = ((s32[32,1,64]{2,1,0:T(1,128)}), s32[32,1,64]{2,1,0:T(1,128)S(1)}, u32[]{:S(2)}, u32[]{:S(2)}) async-start(s32[32,1,64]{2,1,0:T(1,128)} %all_to_all.18), calls=%async_computation | async-start | bytes 32768 | tf_op jit(solution)/shard_map/all_to_all | solution.py:85
  24.9 13.6 %copy-start.3 = (bf16[16,32,256]{2,1,0:T(8,128)(2,1)S(1)}, bf16[16,32,256]{2,1,0:T(8,128)(2,1)}, u32[]{:S(2)}) copy-start(bf16[16,32,256]{2,1,0:T(8,128)(2,1)} %param.13) | copy-start | bytes 786436
  26.2 30.4 %copy-start.1 = (f32[1024,256]{1,0:T(8,128)}, f32[1024,256]{1,0:T(8,128)S(1)}, u32[]{:S(2)}) copy-start(f32[1024,256]{1,0:T(8,128)S(1)} %fusion.106) | copy-start | bytes 3145732
  32.5 31.0 %all-to-all-start.1 = ((bf16[32,64,256]{2,1,0:T(8,128)(2,1)}), bf16[32,64,256]{2,1,0:T(8,128)(2,1)}, u32[]{:S(2)}, u32[]{:S(2)}) async-start(bf16[32,64,256]{2,1,0:T(8,128)(2,1)} %bitcast.103), calls=%async_computation.1 | async-start | bytes 2097152 | tf_op jit(solution)/shard_map/all_to_all | solution.py:78
  38.5 8.3 %collective-permute-start.4 = (bf16[16,1,256]{2,1,0:T(2,128)(2,1)S(1)}, bf16[16,1,256]{2,1,0:T(2,128)(2,1)S(1)}, u32[]{:S(2)}, u32[]{:S(2)}) collective-permute-start(bf16[16,1,256]{2,1,0:T(2,128)(2,1)S(1)} %get-tuple-element.17), channel_id=1, source_target_pairs={{0,4},{4,8},{8,12},{12,16},{16,20},{20,24},{24,28},{28,0},{1,5},{5... | collective-permute-start | bytes 24584 | tf_op jit(solution)/shard_map/ppermute | solution.py:16
  38.7 8.1 %collective-permute-start.5 = (bf16[16,1,256]{2,1,0:T(2,128)(2,1)S(1)}, bf16[16,1,256]{2,1,0:T(2,128)(2,1)S(1)}, u32[]{:S(2)}, u32[]{:S(2)}) collective-permute-start(bf16[16,1,256]{2,1,0:T(2,128)(2,1)S(1)} %get-tuple-element.18), channel_id=1, source_target_pairs={{4,0},{8,4},{12,8},{16,12},{20,16},{24,20},{28,24},{0,28},{5,1},{9... | collective-permute-start | bytes 24584 | tf_op jit(solution)/shard_map/ppermute | solution.py:18
  46.8 9.6 %collective-permute-start.6 = (bf16[1,34,256]{2,1,0:T(8,128)(2,1)S(1)}, bf16[1,34,256]{2,1,0:T(8,128)(2,1)S(1)}, u32[]{:S(2)}, u32[]{:S(2)}) collective-permute-start(bf16[1,34,256]{2,1,0:T(8,128)(2,1)S(1)} %get-tuple-element.15), channel_id=1, source_target_pairs={{0,1},{1,2},{2,3},{4,5},{5,6},{6,7},{8,9},{9,10},{10,11},{12,13},{... | collective-permute-start | bytes 52232 | tf_op jit(solution)/shard_map/ppermute | solution.py:16
  50.1 6.3 %collective-permute-start.7 = (bf16[1,34,256]{2,1,0:T(8,128)(2,1)S(1)}, bf16[1,34,256]{2,1,0:T(8,128)(2,1)S(1)}, u32[]{:S(2)}, u32[]{:S(2)}) collective-permute-start(bf16[1,34,256]{2,1,0:T(8,128)(2,1)S(1)} %get-tuple-element.16), channel_id=1, source_target_pairs={{1,0},{2,1},{3,2},{5,4},{6,5},{7,6},{9,8},{10,9},{11,10},{13,12},{... | collective-permute-start | bytes 52232 | tf_op jit(solution)/shard_map/ppermute | solution.py:18
  63.5 6.8 %copy-start.12 = (pred[8,10]{0,1:T(8,128)(4,1)S(1)}, pred[8,10]{0,1:T(8,128)(4,1)}, u32[]{:S(2)}) copy-start(pred[8,10]{0,1:T(8,128)(4,1)} %constant.65) | copy-start | bytes 244
  68.4 6.4 %collective-permute-start = (bf16[32,2,256]{2,0,1:T(8,128)(2,1)S(1)}, bf16[32,2,256]{2,0,1:T(8,128)(2,1)S(1)}, u32[]{:S(2)}, u32[]{:S(2)}) collective-permute-start(bf16[32,2,256]{2,0,1:T(8,128)(2,1)S(1)} %copy.54), channel_id=1, source_target_pairs={{0,4},{4,8},{8,12},{12,16},{16,20},{20,24},{24,28},{28,0},{1,5},{5... | collective-permute-start | bytes 98312 | tf_op jit(solution)/shard_map/ppermute | solution.py:16
  73.6 2.7 %collective-permute-start.1 = (bf16[32,2,256]{2,0,1:T(8,128)(2,1)S(1)}, bf16[32,2,256]{2,0,1:T(8,128)(2,1)S(1)}, u32[]{:S(2)}, u32[]{:S(2)}) collective-permute-start(bf16[32,2,256]{2,0,1:T(8,128)(2,1)S(1)} %copy.55), channel_id=1, source_target_pairs={{4,0},{8,4},{12,8},{16,12},{20,16},{24,20},{28,24},{0,28},{5,1},{9... | collective-permute-start | bytes 98312 | tf_op jit(solution)/shard_map/ppermute | solution.py:18
  76.5 6.8 %collective-permute-start.2 = (bf16[2,68,256]{2,0,1:T(2,128)(2,1)S(1)}, bf16[2,68,256]{2,0,1:T(2,128)(2,1)S(1)}, u32[]{:S(2)}, u32[]{:S(2)}) collective-permute-start(bf16[2,68,256]{2,0,1:T(2,128)(2,1)S(1)} %get-tuple-element.11), channel_id=1, source_target_pairs={{0,1},{1,2},{2,3},{4,5},{5,6},{6,7},{8,9},{9,10},{10,11},{12,13},{... | collective-permute-start | bytes 208904 | tf_op jit(solution)/shard_map/ppermute | solution.py:16
  81.4 6.2 %collective-permute-start.3 = (bf16[2,68,256]{2,0,1:T(2,128)(2,1)S(1)}, bf16[2,68,256]{2,0,1:T(2,128)(2,1)S(1)}, u32[]{:S(2)}, u32[]{:S(2)}) collective-permute-start(bf16[2,68,256]{2,0,1:T(2,128)(2,1)S(1)} %get-tuple-element.12), channel_id=1, source_target_pairs={{1,0},{2,1},{3,2},{5,4},{6,5},{7,6},{9,8},{10,9},{11,10},{13,12},{... | collective-permute-start | bytes 208904 | tf_op jit(solution)/shard_map/ppermute | solution.py:18
  88.5 1.3 copy-start.9
  88.5 1.3 copy-start.11
  94.1 0.7 copy-start.8
  98.9 0.7 copy-start.10
  104.7 8.4 %copy-start.7 = (s32[1024,1]{0,1:T(1,128)S(1)}, s32[1024,1]{0,1:T(1,128)}, u32[]{:S(2)}) copy-start(s32[1024,1]{0,1:T(1,128)} %copy-done.6) | copy-start | bytes 12292
  110.2 27.7 %all-to-all-start.2 = ((bf16[32,64,256]{2,1,0:T(8,128)(2,1)}), bf16[32,64,256]{2,1,0:T(8,128)(2,1)S(1)}, u32[]{:S(2)}, u32[]{:S(2)}) async-start(bf16[32,64,256]{2,1,0:T(8,128)(2,1)} %bitcast.108), calls=%async_computation.2 | async-start | bytes 2097152 | tf_op jit(solution)/shard_map/all_to_all | solution.py:98
  115.1 1.1 copy-start.2
  137.9 7.1 %copy-start.4 = (bf16[1024,128]{1,0:T(8,128)(2,1)S(1)}, bf16[1024,128]{1,0:T(8,128)(2,1)}, u32[]{:S(2)}) copy-start(bf16[1024,128]{1,0:T(8,128)(2,1)} %param.9) | copy-start | bytes 786436
  142.8 7.5 %copy-start.13 = (pred[8,5]{0,1:T(8,128)(4,1)S(1)}, pred[8,5]{0,1:T(8,128)(4,1)}, u32[]{:S(2)}) copy-start(pred[8,5]{0,1:T(8,128)(4,1)} %constant.63) | copy-start | bytes 124
  146.0 12.8 %all-to-all-start.3 = ((f32[32,4,256]{2,1,0:T(4,128)}), f32[32,4,256]{2,1,0:T(4,128)S(1)}, u32[]{:S(2)}, u32[]{:S(2)}) async-start(f32[32,4,256]{2,1,0:T(4,128)} %reshape.80), calls=%async_computation.3 | async-start | bytes 262144 | tf_op jit(solution)/shard_map/all_to_all | solution.py:113
  150.4 12.5 %copy-start.5 = (bf16[128,256]{1,0:T(8,128)(2,1)S(1)}, bf16[128,256]{1,0:T(8,128)(2,1)}, u32[]{:S(2)}) copy-start(bf16[128,256]{1,0:T(8,128)(2,1)} %param.10) | copy-start | bytes 196612
  159.5 11.0 %all-to-all-start.4 = ((f32[32,4,256]{2,1,0:T(4,128)}), f32[32,4,256]{2,1,0:T(4,128)S(1)}, u32[]{:S(2)}, u32[]{:S(2)}) async-start(f32[32,4,256]{2,1,0:T(4,128)} %broadcast_in_dim.49), calls=%async_computation.4 | async-start | bytes 262144 | tf_op jit(solution)/shard_map/all_to_all | solution.py:116
